TPU v7x, 128 devices: a whole 4x4x4 slice. The times are simulated.
128 devices in a mesh: grp: 8 (over x, core), blk: 16 (over y, z).
Axes of the slice: x: 4, y: 4, z: 4, core: 2. Of those that a mesh axis runs over, the one named last changes fastest.
Arguments:
- features: bfloat16 [8, 16, 4096, 256], P('grp', 'blk'), may hold values from -6 to 6
- hub_rows: int32 [8, 16, 32], P('grp', 'blk'), may hold values from 0 to 4095
- hub_adjacency: bfloat16 [8, 16, 4096, 512], P('grp', 'blk'), as said below
- tile_row: int32 [8, 16, 160], P('grp', 'blk'), may hold values from 0 to 31
- tile_col: int32 [8, 16, 160], P('grp', 'blk'), may hold values from 0 to 63
- tile_count: int32 [8, 16], P('grp', 'blk'), may hold values from 26 to 160, as said below
- tile_values: bfloat16 [8, 16, 160, 128, 128], P('grp', 'blk'), may hold values from 0 to 0.049804688
- send_rows: int32 [8, 16, 8, 16, 32], P('grp', 'blk'), may hold values from 0 to 4095
- weight: bfloat16 [256, 256], replicated, may hold values from -0.375 to 0.375
Outputs:
- activations: bfloat16 [8, 16, 4096, 256], P('grp', 'blk')
Inputs may be any that keep to these rules, and one draw needn't show every extreme that they name: `tile_count`: some device has exactly 160 live tile slots in every draw. `hub_adjacency`: Non-negative edge weights.
All inputs are finite; a program needn't handle non-finite values.
Results may differ from a plain program's by a relative error of at most 0.0014.
The roundings to bfloat16 on the way count: a program that leaves them out, or rounds other values in their place, can miss the bound.
Values may be sent and summed in bfloat16 or wider, within the bound.
No kernel may reach another device: no remote copies, remote signals or barrier semaphores. Data moves between devices by JAX's collectives and lax.ppermute only.
A program may use at most 128 MiB of HBM per device.

v0:
```python
import functools

import jax
import jax.numpy as jnp
from jax import lax
from jax.experimental import pallas as pl
from jax.experimental.pallas import tpu as pltpu
from jax.sharding import PartitionSpec as P

TB = 128


GROUP = 8


def _slot_loop(order_ref, rows_ref, cols_ref, start, n, table_ref, vals_ref, acc_ref, lo):
    width = table_ref.shape[0] // TB

    def body(g, carry):
        for j in range(GROUP):
            p = g * GROUP + j
            t = order_ref[start + jnp.minimum(p, n - 1)]
            c = jnp.clip(cols_ref[t] - lo, 0, width - 1)
            r0 = pl.multiple_of(rows_ref[t] * TB, TB)
            c0 = pl.multiple_of(c * TB, TB)
            prod = jnp.dot(vals_ref[t], table_ref[pl.ds(c0, TB), :], preferred_element_type=jnp.float32)
            acc_ref[pl.ds(r0, TB), :] += jnp.where(p < n, prod, 0.0)
        return carry

    lax.fori_loop(0, (n + GROUP - 1) // GROUP, body, 0)


def _local_kernel(order_ref, rows_ref, cols_ref, counts_ref, table_ref, vals_ref, adj_ref, hub_ref,
                  acc_ref):
    n = acc_ref.shape[0]
    blk = 512
    for i in range(n // blk):
        sl = pl.ds(i * blk, blk)
        acc_ref[sl, :] = jnp.dot(adj_ref[sl, :], hub_ref[...], preferred_element_type=jnp.float32)
    _slot_loop(order_ref, rows_ref, cols_ref, 0, counts_ref[0], table_ref, vals_ref, acc_ref, 0)


def _remote_kernel(order_ref, rows_ref, cols_ref, counts_ref, table_ref, vals_hbm, acc_ref, w_ref,
                   out_ref, vbuf, sems, *, lo):
    s = pl.program_id(0)

    @pl.when(s == 0)
    def _():
        start = counts_ref[0]
        n = counts_ref[1]
        groups = (n + GROUP - 1) // GROUP
        width = table_ref.shape[0] // TB

        def issue(g):
            for j in range(GROUP):
                p = g * GROUP + j
                t = order_ref[start + jnp.minimum(p, n - 1)]
                pltpu.make_async_copy(vals_hbm.at[t], vbuf.at[p], sems.at[g]).start()

        @pl.when(groups > 0)
        def _():
            issue(0)

        def body(g, carry):
            @pl.when(g + 1 < groups)
            def _():
                issue(g + 1)

            base = pl.multiple_of(g * GROUP, GROUP)
            pltpu.make_async_copy(
                vals_hbm.at[pl.ds(0, GROUP)], vbuf.at[pl.ds(base, GROUP)], sems.at[g]
            ).wait()
            for j in range(GROUP):
                p = g * GROUP + j
                t = order_ref[start + jnp.minimum(p, n - 1)]
                c = jnp.clip(cols_ref[t] - lo, 0, width - 1)
                r0 = pl.multiple_of(rows_ref[t] * TB, TB)
                c0 = pl.multiple_of(c * TB, TB)
                prod = jnp.dot(vbuf[p], table_ref[pl.ds(c0, TB), :], preferred_element_type=jnp.float32)
                acc_ref[pl.ds(r0, TB), :] += jnp.where(p < n, prod, 0.0)
            return carry

        lax.fori_loop(0, groups, body, 0)

    @pl.when(s > 0)
    def _():
        blk = out_ref.shape[0]
        r0 = pl.multiple_of((s - 1) * blk, blk)
        agg = acc_ref[pl.ds(r0, blk), :].astype(jnp.bfloat16)
        mixed = jnp.dot(agg, w_ref[...], preferred_element_type=jnp.float32)
        out_ref[...] = jnp.maximum(mixed, 0.0).astype(out_ref.dtype)


def local_tiles(order, rows, cols, counts, table, vals, adj, hub):
    n, width = table.shape
    const2 = lambda s, *_: (0, 0)
    const3 = lambda s, *_: (0, 0, 0)
    return pl.pallas_call(
        _local_kernel,
        grid_spec=pltpu.PrefetchScalarGridSpec(
            num_scalar_prefetch=4,
            grid=(1,),
            in_specs=[
                pl.BlockSpec((n, width), const2),
                pl.BlockSpec(vals.shape, const3),
                pl.BlockSpec(adj.shape, const2),
                pl.BlockSpec(hub.shape, const2),
            ],
            out_specs=pl.BlockSpec((n, width), const2),
        ),
        out_shape=jax.ShapeDtypeStruct((n, width), jnp.float32),
    )(order, rows, cols, counts, table, vals, adj, hub)


def remote_tiles(order, rows, cols, counts, table, vals, part, weight, lo):
    n, width = part.shape
    blk = 1024
    fin_steps = n // blk
    const2 = lambda s, *_: (0, 0)
    const3 = lambda s, *_: (0, 0, 0)
    fin = lambda s, *_: (jnp.maximum(s - 1, 0), 0)
    return pl.pallas_call(
        functools.partial(_remote_kernel, lo=lo),
        grid_spec=pltpu.PrefetchScalarGridSpec(
            num_scalar_prefetch=4,
            grid=(1 + fin_steps,),
            in_specs=[
                pl.BlockSpec(table.shape, const2),
                pl.BlockSpec(memory_space=pl.ANY),
                pl.BlockSpec((n, width), const2),
                pl.BlockSpec(weight.shape, const2),
            ],
            out_specs=pl.BlockSpec((blk, width), fin),
            scratch_shapes=[
                pltpu.VMEM(vals.shape, vals.dtype),
                pltpu.SemaphoreType.DMA((vals.shape[0] // GROUP,)),
            ],
        ),
        out_shape=jax.ShapeDtypeStruct((n, width), jnp.bfloat16),
    )(order, rows, cols, counts, table, vals, part, weight)


def slot_order(cols, count, width):
    slots = cols.shape[0]
    t = jnp.arange(slots, dtype=jnp.int32)
    live = t < count
    is_a = live & (cols < width)
    is_b = live & (cols >= width)
    dead = ~live
    n_a = jnp.sum(is_a.astype(jnp.int32))
    n_b = jnp.sum(is_b.astype(jnp.int32))
    pos = jnp.where(
        is_a,
        jnp.cumsum(is_a.astype(jnp.int32)) - 1,
        jnp.where(
            is_b,
            n_a + jnp.cumsum(is_b.astype(jnp.int32)) - 1,
            n_a + n_b + jnp.cumsum(dead.astype(jnp.int32)) - 1,
        ),
    )
    order = jnp.sum(jnp.where(pos[None, :] == t[:, None], t[None, :], 0), axis=1).astype(jnp.int32)
    return order, jnp.stack([n_a, n_b]).astype(jnp.int32)


def _gather_kernel(send_ref, feat_ref, out_ref, src_ref, dst_ref):
    n = feat_ref.shape[0]
    chunk = 512
    for i in range(n // chunk):
        sl = pl.ds(i * chunk, chunk)
        src_ref[sl, :] = feat_ref[sl, :].astype(jnp.float32)

    def body(g, carry):
        base = pl.multiple_of(g * 8, 8)
        rows = [src_ref[pl.ds(send_ref[base + k], 1), :] for k in range(8)]
        dst_ref[pl.ds(base, 8), :] = jnp.concatenate(rows, axis=0)
        return carry

    lax.fori_loop(0, out_ref.shape[0] // 8, body, 0)
    for i in range(out_ref.shape[0] // chunk):
        sl = pl.ds(i * chunk, chunk)
        out_ref[sl, :] = dst_ref[sl, :].astype(out_ref.dtype)


def gather_rows(send_idx, feat):
    n, width = feat.shape
    m = send_idx.shape[0]
    return pl.pallas_call(
        _gather_kernel,
        grid_spec=pltpu.PrefetchScalarGridSpec(
            num_scalar_prefetch=1,
            grid=(1,),
            in_specs=[pl.BlockSpec((n, width), lambda s, *_: (0, 0))],
            out_specs=pl.BlockSpec((m, width), lambda s, *_: (0, 0)),
            scratch_shapes=[pltpu.VMEM((n, width), jnp.float32), pltpu.VMEM((m, width), jnp.float32)],
        ),
        out_shape=jax.ShapeDtypeStruct((m, width), feat.dtype),
    )(send_idx, feat)


def per_device(
    features,
    hub_rows,
    hub_adjacency,
    tile_row,
    tile_col,
    tile_count,
    tile_values,
    send_rows,
    weight,
):
    local = features[0, 0]
    rows = local.shape[0]
    adjacency = hub_adjacency[0, 0]
    n_blk = lax.axis_size("blk")
    hub_block = local[hub_rows[0, 0]]
    copies = jnp.broadcast_to(hub_block[None], (n_blk,) + hub_block.shape)
    hub_group = lax.all_to_all(copies, "blk", split_axis=0, concat_axis=0, tiled=True)
    hub_group = hub_group.reshape(-1, local.shape[-1])
    listing = send_rows[0, 0]
    outgoing = gather_rows(listing.reshape(-1), local)
    incoming = lax.all_to_all(outgoing, ("grp", "blk"), split_axis=0, concat_axis=0, tiled=True)
    t_rows = tile_row[0, 0]
    t_cols = tile_col[0, 0]
    vals = tile_values[0, 0]
    order, counts = slot_order(t_cols, tile_count[0, 0], rows // TB)
    part = local_tiles(order, t_rows, t_cols, counts, local, vals, adjacency, hub_group)
    out = remote_tiles(order, t_rows, t_cols, counts, incoming, vals, part, weight, rows // TB)
    return out[None, None]


def solution(mesh):
    return jax.shard_map(
        per_device,
        mesh=mesh,
        in_specs=(
            P("grp", "blk", None, None),
            P("grp", "blk", None),
            P("grp", "blk", None, None),
            P("grp", "blk", None),
            P("grp", "blk", None),
            P("grp", "blk"),
            P("grp", "blk", None, None, None),
            P("grp", "blk", None, None, None),
            P(),
        ),
        out_specs=P("grp", "blk", None, None),
        check_vma=False,
    )
```

profile of v0, /device:TPU:1, one launch (start us, length us, event | category | flops | bytes accessed | tf_op | source)
XLA Modules:
  0.0 83.9 jit_solution(8092561700267545864)
XLA Ops:
  0.0 0.7 fusion.2
  0.7 2.5 %gather_fusion = bf16[32,256]{1,0:T(8,128)(2,1)S(1)} fusion(bf16[4096,256]{1,0:T(8,128)(2,1)} %bitcast.34, s32[1024]{0:T(1024)S(1)} %pad_clamp_fusion), kind=kCustom, calls=%fused_computation | custom fusion | bytes 32896 | tf_op jit(solution)/shard_map/gather | solution.py:215
  3.1 0.7 broadcast_in_dim.27
  3.9 8.6 %all-to-all-start.1 = ((bf16[16,32,256]{2,1,0:T(8,128)(2,1)}), bf16[16,32,256]{2,1,0:T(8,128)(2,1)S(1)}, u32[]{:S(2)}, u32[]{:S(2)}) async-start(bf16[16,32,256]{2,1,0:T(8,128)(2,1)} %broadcast_in_dim.27), calls=%async_computation.1 | async-start | bytes 524288 | tf_op jit(solution)/shard_map/all_to_all | solution.py:217
  12.5 1.5 %reshape_squeeze.3.send_ref = s32[4096]{0:T(1024)} reshape(s32[1,1,8,16,32]{4,3,2,1,0:T(8,128)} %param.16) | data formatting | bytes 32768 | tf_op jit(solution)/shard_map/reshape;squeeze | solution.py:220
  14.0 14.8 %shard_map.91 = bf16[4096,256]{1,0:T(8,128)(2,1)} custom-call(s32[4096]{0:T(1024)} %reshape_squeeze.3.send_ref, bf16[4096,256]{1,0:T(8,128)(2,1)} %bitcast.35), custom_call_target="tpu_custom_call" | custom-call | tf_op jit(solution)/shard_map/pallas_call | solution.py:187
  28.8 0.0 all-to-all-done.1
  28.8 0.0 copy-start.1
  28.8 0.0 copy-start.2
  28.8 0.7 copy-done.1
  29.5 10.1 %all-to-all-start = ((bf16[128,32,256]{2,1,0:T(8,128)(2,1)}), bf16[128,32,256]{2,1,0:T(8,128)(2,1)S(1)}, u32[]{:S(2)}, u32[]{:S(2)}) async-start(bf16[128,32,256]{2,1,0:T(8,128)(2,1)} %bitcast.38), calls=%async_computation | async-start | bytes 4194304 | tf_op jit(solution)/shard_map/all_to_all | solution.py:221
  40.3 0.3 reduce-window.37
  40.6 0.1 slice.36
  40.7 0.0 copy-done.2
  40.7 0.7 convert_reduce_fusion
  41.4 0.3 reduce-window.29
  41.7 0.1 slice.33
  41.9 0.3 reduce-window.25
  42.2 0.1 slice.30
  43.5 1.9 %pad_add_fusion.counts_ref = s32[2]{0:T(128)} fusion(s32[1]{0:T(128)} %bitcast.10, s32[1]{0:T(128)} %bitcast.9), kind=kLoop, calls=%fused_computation.21 | loop fusion | flops 2 | bytes 16 | tf_op jit(solution)/shard_map/stack | solution.py:162
  45.4 0.1 slice_reduce_fusion
  45.5 0.1 slice_reduce_fusion.1
  45.6 0.1 slice_reduce_fusion.2
  45.8 0.1 add_bitcast_fusion.2
  45.8 0.1 add_bitcast_fusion
  45.9 0.7 select_select_fusion
  46.6 0.6 select_reduce_fusion.order_ref
  47.3 11.3 %shard_map.92.acc_ref = f32[4096,256]{1,0:T(8,128)} custom-call(s32[160]{0:T(256)} %select_reduce_fusion.order_ref, s32[160]{0:T(256)} %bitcast.44, s32[160]{0:T(256)} %bitcast.41, s32[2]{0:T(128)} %pad_add_fusion.counts_ref, bf16[4096,256]{1,0:T(8,128)(2,1)} %bitcast.36, bf16[160,128,128]{2,1,0:T(8,128)(2,1)} %bitcast.32, bf16[4096,512]{1,0:T(8,128)(2,1)} %bitcast.39, ...), custom_call_target="tpu_custom_call" | custom-call | tf_op jit(solution)/shard_map/pallas_call | solution.py:98
  58.6 10.5 %all-to-all-done = bf16[128,32,256]{2,1,0:T(8,128)(2,1)S(1)} async-done(((bf16[128,32,256]{2,1,0:T(8,128)(2,1)}), bf16[128,32,256]{2,1,0:T(8,128)(2,1)S(1)}, u32[]{:S(2)}, u32[]{:S(2)}) %all-to-all-start) | async-done | bytes 2097184 | tf_op jit(solution)/shard_map/all_to_all | solution.py:221
  69.1 0.0 copy-start
  69.1 1.3 %copy-done = bf16[128,32,256]{2,1,0:T(8,128)(2,1)} copy-done((bf16[128,32,256]{2,1,0:T(8,128)(2,1)}, bf16[128,32,256]{2,1,0:T(8,128)(2,1)S(1)}, u32[]{:S(2)}) %copy-start) | copy-done | bytes 2097176
  70.4 13.5 %shard_map.93 = bf16[4096,256]{1,0:T(8,128)(2,1)} custom-call(s32[160]{0:T(256)} %select_reduce_fusion.order_ref, s32[160]{0:T(256)} %bitcast.45, s32[160]{0:T(256)} %bitcast.42, s32[2]{0:T(128)} %pad_add_fusion.counts_ref, bf16[4096,256]{1,0:T(8,128)(2,1)} %bitcast.37, bf16[160,128,128]{2,1,0:T(8,128)(2,1)} %bitcast.33, f32[4096,256]{1,0:T(8,128)} %shard_map.92.acc_ref, ...), custom_call_target="tpu_custom_call" | custom-call | tf_op jit(solution)/shard_map/pallas_call | solution.py:122
  (10 shorter events, 0.1 us)
Async XLA Ops:
  3.9 24.9 %all-to-all-start.1 = ((bf16[16,32,256]{2,1,0:T(8,128)(2,1)}), bf16[16,32,256]{2,1,0:T(8,128)(2,1)S(1)}, u32[]{:S(2)}, u32[]{:S(2)}) async-start(bf16[16,32,256]{2,1,0:T(8,128)(2,1)} %broadcast_in_dim.27), calls=%async_computation.1 | async-start | bytes 524288 | tf_op jit(solution)/shard_map/all_to_all | solution.py:217
  28.8 0.7 copy-start.1
  28.8 11.9 %copy-start.2 = (s32[1,1,160]{2,1,0:T(1,128)S(1)}, s32[1,1,160]{2,1,0:T(1,128)}, u32[]{:S(2)}) copy-start(s32[1,1,160]{2,1,0:T(1,128)} %param.13) | copy-start | bytes 1924
  29.5 39.6 %all-to-all-start = ((bf16[128,32,256]{2,1,0:T(8,128)(2,1)}), bf16[128,32,256]{2,1,0:T(8,128)(2,1)S(1)}, u32[]{:S(2)}, u32[]{:S(2)}) async-start(bf16[128,32,256]{2,1,0:T(8,128)(2,1)} %bitcast.38), calls=%async_computation | async-start | bytes 4194304 | tf_op jit(solution)/shard_map/all_to_all | solution.py:221
  69.1 1.3 %copy-start = (bf16[128,32,256]{2,1,0:T(8,128)(2,1)}, bf16[128,32,256]{2,1,0:T(8,128)(2,1)S(1)}, u32[]{:S(2)}) copy-start(bf16[128,32,256]{2,1,0:T(8,128)(2,1)S(1)} %all-to-all-done) | copy-start | bytes 6291460
where the time goes:
time: 83.9 us
  Pallas kernels  39.6 us (47%)
  starting transfers between devices  18.7 us (22%)
  waiting for transfers between devices  10.5 us (13%)
  local copies, waits for them, and re-layouts  7.3 us (9%)
  other arithmetic  5.79 us (7%)
  between operations  1.97 us (2%)
    pallas_call x1, Pallas kernels, gather_rows(): pl.pallas_call(_gather_kernel, grid_spec=pltpu.PrefetchScalarGridSpec(num...  14.8 us
    pallas_call x1, Pallas kernels, remote_tiles(): pl.pallas_call(functools.partial(_remote_kernel, lo=lo), grid_spec=pltpu....  13.5 us
    pallas_call x1, Pallas kernels, local_tiles(): pl.pallas_call(_local_kernel, grid_spec=pltpu.PrefetchScalarGridSpec(num_...  11.3 us
    all_to_all x1, waiting for transfers between devices, per_device(): lax.all_to_all(outgoing, ('grp', 'blk'), split_axis=0, concat_axis=0, til...  10.5 us
    all_to_all x1, starting transfers between devices, per_device(): lax.all_to_all(outgoing, ('grp', 'blk'), split_axis=0, concat_axis=0, til...  10.1 us
    all_to_all x1, starting transfers between devices, per_device(): lax.all_to_all(copies, 'blk', split_axis=0, concat_axis=0, tiled=True)  8.6 us
    gather x1, local copies, waits for them, and re-layouts, per_device(): hub_block = local[hub_rows[0, 0]]  2.46 us
    unnamed x6, local copies, waits for them, and re-layouts  2.02 us
  transfers between devices with their start and end apart: 2, of which 1 were waited for; matrix products, arithmetic and copies ran while one was open for 9% of the time, Pallas kernels for 31%

commit v1 on v0

--- a/solution.py
+++ b/solution.py
@@ -40,22 +40,21 @@
     _slot_loop(order_ref, rows_ref, cols_ref, 0, counts_ref[0], table_ref, vals_ref, acc_ref, 0)
 
 
-def _remote_kernel(order_ref, rows_ref, cols_ref, counts_ref, table_ref, vals_hbm, acc_ref, w_ref,
-                   out_ref, vbuf, sems, *, lo):
+def _remote_kernel(order_ref, rows_ref, cols_ref, counts_ref, pslot_ref, pvalid_ref, table_ref,
+                   vals_hbm, acc_ref, w_ref, out_ref, vbuf, sems, *, lo):
     s = pl.program_id(0)
 
     @pl.when(s == 0)
     def _():
-        start = counts_ref[0]
-        n = counts_ref[1]
-        groups = (n + GROUP - 1) // GROUP
+        npairs = counts_ref[2]
+        per = GROUP // 2
+        groups = (npairs + per - 1) // per
         width = table_ref.shape[0] // TB
 
         def issue(g):
             for j in range(GROUP):
                 p = g * GROUP + j
-                t = order_ref[start + jnp.minimum(p, n - 1)]
-                pltpu.make_async_copy(vals_hbm.at[t], vbuf.at[p], sems.at[g]).start()
+                pltpu.make_async_copy(vals_hbm.at[pslot_ref[p]], vbuf.at[p], sems.at[g]).start()
 
         @pl.when(groups > 0)
         def _():
@@ -70,14 +69,20 @@
             pltpu.make_async_copy(
                 vals_hbm.at[pl.ds(0, GROUP)], vbuf.at[pl.ds(base, GROUP)], sems.at[g]
             ).wait()
-            for j in range(GROUP):
-                p = g * GROUP + j
-                t = order_ref[start + jnp.minimum(p, n - 1)]
-                c = jnp.clip(cols_ref[t] - lo, 0, width - 1)
-                r0 = pl.multiple_of(rows_ref[t] * TB, TB)
-                c0 = pl.multiple_of(c * TB, TB)
-                prod = jnp.dot(vbuf[p], table_ref[pl.ds(c0, TB), :], preferred_element_type=jnp.float32)
-                acc_ref[pl.ds(r0, TB), :] += jnp.where(p < n, prod, 0.0)
+            for j in range(per):
+                q = g * per + j
+                pa = 2 * q
+                pb = pa + 1
+                ta = pslot_ref[pa]
+                tb = pslot_ref[pb]
+                ca = pl.multiple_of(jnp.clip(cols_ref[ta] - lo, 0, width - 1) * TB, TB)
+                cb = pl.multiple_of(jnp.clip(cols_ref[tb] - lo, 0, width - 1) * TB, TB)
+                r0 = pl.multiple_of(rows_ref[ta] * TB, TB)
+                vb = jnp.where(pvalid_ref[pb] > 0, vbuf[pb], jnp.zeros_like(vbuf[pb]))
+                lhs = jnp.concatenate([vbuf[pa], vb], axis=1)
+                rhs = jnp.concatenate([table_ref[pl.ds(ca, TB), :], table_ref[pl.ds(cb, TB), :]], axis=0)
+                prod = jnp.dot(lhs, rhs, preferred_element_type=jnp.float32)
+                acc_ref[pl.ds(r0, TB), :] += jnp.where(q < npairs, prod, 0.0)
             return carry
 
         lax.fori_loop(0, groups, body, 0)
@@ -112,7 +117,7 @@
     )(order, rows, cols, counts, table, vals, adj, hub)
 
 
-def remote_tiles(order, rows, cols, counts, table, vals, part, weight, lo):
+def remote_tiles(order, rows, cols, counts, pslot, pvalid, table, vals, part, weight, lo):
     n, width = part.shape
     blk = 1024
     fin_steps = n // blk
@@ -122,7 +127,7 @@
     return pl.pallas_call(
         functools.partial(_remote_kernel, lo=lo),
         grid_spec=pltpu.PrefetchScalarGridSpec(
-            num_scalar_prefetch=4,
+            num_scalar_prefetch=6,
             grid=(1 + fin_steps,),
             in_specs=[
                 pl.BlockSpec(table.shape, const2),
@@ -132,15 +137,15 @@
             ],
             out_specs=pl.BlockSpec((blk, width), fin),
             scratch_shapes=[
-                pltpu.VMEM(vals.shape, vals.dtype),
-                pltpu.SemaphoreType.DMA((vals.shape[0] // GROUP,)),
+                pltpu.VMEM((pslot.shape[0],) + vals.shape[1:], vals.dtype),
+                pltpu.SemaphoreType.DMA((pslot.shape[0] // GROUP,)),
             ],
         ),
         out_shape=jax.ShapeDtypeStruct((n, width), jnp.bfloat16),
-    )(order, rows, cols, counts, table, vals, part, weight)
-
-
-def slot_order(cols, count, width):
+    )(order, rows, cols, counts, pslot, pvalid, table, vals, part, weight)
+
+
+def slot_order(rows, cols, count, width, rows_total):
     slots = cols.shape[0]
     t = jnp.arange(slots, dtype=jnp.int32)
     live = t < count
@@ -159,7 +164,26 @@
         ),
     )
     order = jnp.sum(jnp.where(pos[None, :] == t[:, None], t[None, :], 0), axis=1).astype(jnp.int32)
-    return order, jnp.stack([n_a, n_b]).astype(jnp.int32)
+    nrow = rows_total
+    rr = jnp.arange(nrow, dtype=jnp.int32)
+    hit = is_b[None, :] & (rows[None, :] == rr[:, None])
+    cnt = jnp.sum(hit.astype(jnp.int32), axis=1)
+    pairs = (cnt + 1) // 2
+    pair_off = jnp.cumsum(pairs) - pairs
+    same = is_b[None, :] & (rows[None, :] == rows[:, None]) & (t[None, :] < t[:, None])
+    rank = jnp.sum(same.astype(jnp.int32), axis=1)
+    ppos = jnp.where(is_b, 2 * pair_off[rows] + rank, -1)
+    npos = 2 * (slots + nrow) // 2
+    npos = ((npos + GROUP - 1) // GROUP) * GROUP
+    p = jnp.arange(npos, dtype=jnp.int32)
+    at = ppos[None, :] == p[:, None]
+    pvalid = jnp.any(at, axis=1)
+    pslot = jnp.sum(jnp.where(at, t[None, :], 0), axis=1).astype(jnp.int32)
+    partner = jnp.concatenate([pslot[:1], pslot[:-1]])
+    pslot = jnp.where(pvalid, pslot, jnp.where(p % 2 == 1, partner, 0)).astype(jnp.int32)
+    npairs = jnp.sum(pairs).astype(jnp.int32)
+    counts = jnp.stack([n_a, n_b, npairs]).astype(jnp.int32)
+    return order, counts, pslot, pvalid.astype(jnp.int32)
 
 
 def _gather_kernel(send_ref, feat_ref, out_ref, src_ref, dst_ref):
@@ -222,9 +246,9 @@
     t_rows = tile_row[0, 0]
     t_cols = tile_col[0, 0]
     vals = tile_values[0, 0]
-    order, counts = slot_order(t_cols, tile_count[0, 0], rows // TB)
+    order, counts, pslot, pvalid = slot_order(t_rows, t_cols, tile_count[0, 0], rows // TB, rows // TB)
     part = local_tiles(order, t_rows, t_cols, counts, local, vals, adjacency, hub_group)
-    out = remote_tiles(order, t_rows, t_cols, counts, incoming, vals, part, weight, rows // TB)
+    out = remote_tiles(order, t_rows, t_cols, counts, pslot, pvalid, incoming, vals, part, weight, rows // TB)
     return out[None, None]
 
 

time: 83.9 us -> 104 us (1.24)
  the two profiles are of different devices: /device:TPU:1 before, /device:TPU:83 now
where the time goes in v1:
time: 104 us; the launch traced here: 101 us
  Pallas kernels  40.7 us (39%)
  other arithmetic  31.9 us (31%)
  starting transfers between devices  17.5 us (17%)
  local copies, waits for them, and re-layouts  9.34 us (9%)
  between operations  2.05 us (2%)
    select_n x1, other arithmetic, slot_order(): ppos = jnp.where(is_b, 2 * pair_off[rows] + rank, -1)  15.7 us
    pallas_call x1, Pallas kernels, remote_tiles(): pl.pallas_call(functools.partial(_remote_kernel, lo=lo), grid_spec=pltpu....  14.9 us
    pallas_call x1, Pallas kernels, gather_rows(): pl.pallas_call(_gather_kernel, grid_spec=pltpu.PrefetchScalarGridSpec(num...  14.8 us
    pallas_call x1, Pallas kernels, local_tiles(): pl.pallas_call(_local_kernel, grid_spec=pltpu.PrefetchScalarGridSpec(num_...  11 us
    all_to_all x1, starting transfers between devices, per_device(): lax.all_to_all(outgoing, ('grp', 'blk'), split_axis=0, concat_axis=0, til...  10.6 us
    all_to_all x1, starting transfers between devices, per_device(): lax.all_to_all(copies, 'blk', split_axis=0, concat_axis=0, tiled=True)  6.83 us
    gather x2, other arithmetic, slot_order(): ppos = jnp.where(is_b, 2 * pair_off[rows] + rank, -1)  5.18 us
    another operation x1, other arithmetic, slot_order(): counts = jnp.stack([n_a, n_b, npairs]).astype(jnp.int32)  2.56 us
  transfers between devices with their start and end apart: 2, of which 0 were waited for; matrix products, arithmetic and copies ran while one was open for 35% of the time, Pallas kernels for 25%

profile of v1, /device:TPU:83, one launch (start us, length us, event | category | flops | bytes accessed | tf_op | source)
XLA Modules:
  0.0 101.5 jit_solution(1116652991220564011)
XLA Ops:
  0.0 0.7 fusion.8
  0.7 2.5 %gather_fusion = bf16[32,256]{1,0:T(8,128)(2,1)S(1)} fusion(bf16[4096,256]{1,0:T(8,128)(2,1)} %bitcast.80, s32[1024]{0:T(1024)S(1)} %pad_clamp_fusion), kind=kCustom, calls=%fused_computation | custom fusion | bytes 32896 | tf_op jit(solution)/shard_map/gather | solution.py:239
  3.1 0.7 broadcast_in_dim.57
  3.9 6.8 %all-to-all-start.1 = ((bf16[16,32,256]{2,1,0:T(8,128)(2,1)}), bf16[16,32,256]{2,1,0:T(8,128)(2,1)S(1)}, u32[]{:S(2)}, u32[]{:S(2)}) async-start(bf16[16,32,256]{2,1,0:T(8,128)(2,1)} %broadcast_in_dim.57), calls=%async_computation.1 | async-start | bytes 524288 | tf_op jit(solution)/shard_map/all_to_all | solution.py:241
  11.4 1.4 %convert_reduce_fusion.2 = (s32[]{:T(128)}, pred[160]{0:T(512)(128)(4,1)S(1)}, s32[]{:T(128)}, pred[160]{0:T(512)(128)(4,1)S(1)}) fusion(s32[160]{0:T(256)} %bitcast.92, s32[]{:T(128)} %bitcast.77), kind=kLoop, calls=%fused_computation.78 | loop fusion | flops 1438 | bytes 972 | tf_op jit(solution)/shard_map/reduce_sum | solution.py:156
  12.8 0.8 convert_reduce_fusion.1
  13.6 0.1 copy.12
  13.7 0.1 reduce-window.48
  13.7 0.1 reduce.4
  13.9 0.7 fusion.11
  14.6 5.1 %compare_select_fusion.1 = (s32[160,1]{0,1:T(1,128)S(1)}, s32[160,1]{0,1:T(1,128)S(1)}) fusion(s32[]{:T(128)} %bitcast.39, s32[]{:T(128)} %bitcast.40, s32[]{:T(128)} %bitcast.41, s32[]{:T(128)} %bitcast.42, s32[]{:T(128)} %bitcast.43, s32[]{:T(128)} %bitcast.45, s32[]{:T(128)} %bitcast.44, s32[1,1,160]{2,1,0:T(1,128)} %param.12), kind=kLoop, calls=%fused_computation.39 | loop fusion | flops 2400 | bytes 1948 | tf_op jit(solution)/shard_map/gather | solution.py:175
  19.7 1.5 %reshape_squeeze.3.send_ref = s32[4096]{0:T(1024)} reshape(s32[1,1,8,16,32]{4,3,2,1,0:T(8,128)} %param.16) | data formatting | bytes 32768 | tf_op jit(solution)/shard_map/reshape;squeeze | solution.py:244
  21.2 14.8 %shard_map.91 = bf16[4096,256]{1,0:T(8,128)(2,1)} custom-call(s32[4096]{0:T(1024)} %reshape_squeeze.3.send_ref, bf16[4096,256]{1,0:T(8,128)(2,1)} %bitcast.81), custom_call_target="tpu_custom_call" | custom-call | tf_op jit(solution)/shard_map/pallas_call | solution.py:211
  36.0 0.7 fusion.10
  36.7 0.1 compare_reduce_fusion.24
  36.8 0.0 all-to-all-done.1
  36.8 0.0 copy-start.1
  36.8 0.0 copy-start.2
  36.9 0.7 copy-done.1
  37.5 10.6 %all-to-all-start = ((bf16[128,32,256]{2,1,0:T(8,128)(2,1)}), bf16[128,32,256]{2,1,0:T(8,128)(2,1)S(1)}, u32[]{:S(2)}, u32[]{:S(2)}) async-start(bf16[128,32,256]{2,1,0:T(8,128)(2,1)} %bitcast.83), calls=%async_computation | async-start | bytes 4194304 | tf_op jit(solution)/shard_map/all_to_all | solution.py:245
  48.2 0.3 reduce-window.46
  48.5 0.1 slice.42
  48.6 0.3 reduce-window.42
  48.9 0.1 slice.36
  49.0 0.3 reduce-window.44
  49.3 0.1 slice.39
  49.4 0.7 reduce_sum.67
  50.2 0.0 copy-done.2
  50.2 0.2 convert_reduce_fusion
  50.3 15.7 %fusion.6 = s32[160]{0:T(256)S(1)} fusion(pred[160]{0:T(512)(128)(4,1)S(1)} %get-tuple-element.35, s32[160]{0:T(256)S(1)} %convert_reduce_fusion, pred[160]{0:T(512)(128)(4,1)S(1)} %get-tuple-element.29, pred[160]{0:T(512)(128)(4,1)S(1)} %get-tuple-element.28, pred[160]{0:T(512)(128)(4,1)S(1)} %get-tuple-element.27, pred[160]{0:T(512)(128)(4,1)S(1)} %get-tuple-element.26, ...), kind=kLoop, calls=%fused_computation.63 | loop fusion | flops 4480 | bytes 6180 | tf_op jit(solution)/shard_map/jit(_where)/select_n | solution.py:175
  66.1 0.1 select_reduce_fusion
  66.2 0.6 slice.45
  66.7 0.1 fusion
  66.8 0.5 convert_element_type.22.pvalid_ref
  68.6 2.6 %pad_add_fusion.counts_ref = s32[3]{0:T(128)} fusion(s32[1]{0:T(128)} %bitcast.11, s32[1]{0:T(128)} %bitcast.10, s32[1]{0:T(128)} %bitcast.9), kind=kLoop, calls=%fused_computation.76 | loop fusion | flops 6 | bytes 24 | tf_op jit(solution)/shard_map/stack | solution.py:185
  71.2 0.1 slice_reduce_fusion
  71.3 0.1 slice_reduce_fusion.2
  71.4 0.1 slice_reduce_fusion.1
  71.5 0.1 add_bitcast_fusion.2
  71.6 0.1 add_bitcast_fusion
  71.7 0.6 select_select_fusion
  72.3 0.7 select_reduce_fusion.1.order_ref
  73.0 1.3 %fusion.4.pslot_ref = s32[192]{0:T(256)} fusion(pred[192]{0:T(512)(128)(4,1)S(1)} %fusion, s32[192]{0:T(256)S(1)} %select_reduce_fusion, s32[191]{0:T(256)S(1)} %bitcast.91, s32[1]{0:T(128)} %slice.45), kind=kLoop, calls=%fused_computation.60 | loop fusion | flops 1920 | bytes 2496 | tf_op jit(solution)/shard_map/jit(_where)/select_n | solution.py:183
  74.2 11.0 %shard_map.92.acc_ref = f32[4096,256]{1,0:T(8,128)} custom-call(s32[160]{0:T(256)} %select_reduce_fusion.1.order_ref, s32[160]{0:T(256)} %bitcast.88, s32[160]{0:T(256)} %bitcast.93, s32[3]{0:T(128)} %pad_add_fusion.counts_ref, bf16[4096,256]{1,0:T(8,128)(2,1)} %bitcast.82, bf16[160,128,128]{2,1,0:T(8,128)(2,1)} %bitcast.78, bf16[4096,512]{1,0:T(8,128)(2,1)} %bitcast.85, ...), custom_call_target="tpu_custom_call" | custom-call | tf_op jit(solution)/shard_map/pallas_call | solution.py:103
  85.2 0.0 all-to-all-done
  85.3 0.0 copy-start
  85.3 1.3 %copy-done = bf16[128,32,256]{2,1,0:T(8,128)(2,1)} copy-done((bf16[128,32,256]{2,1,0:T(8,128)(2,1)}, bf16[128,32,256]{2,1,0:T(8,128)(2,1)S(1)}, u32[]{:S(2)}) %copy-start) | copy-done | bytes 2097176
  86.6 14.9 %shard_map.93 = bf16[4096,256]{1,0:T(8,128)(2,1)} custom-call(s32[160]{0:T(256)} %select_reduce_fusion.1.order_ref, s32[160]{0:T(256)} %bitcast.89, s32[160]{0:T(256)} %bitcast.94, s32[3]{0:T(128)} %pad_add_fusion.counts_ref, s32[192]{0:T(256)} %fusion.4.pslot_ref, s32[192]{0:T(256)} %convert_element_type.22.pvalid_ref, bf16[4096,256]{1,0:T(8,128)(2,1)} %bitcast.84, ...), custom_call_target="tpu_custom_call" | custom-call | tf_op jit(solution)/shard_map/pallas_call | solution.py:127
  (12 shorter events, 0.2 us)
Async XLA Ops:
  3.9 33.0 %all-to-all-start.1 = ((bf16[16,32,256]{2,1,0:T(8,128)(2,1)}), bf16[16,32,256]{2,1,0:T(8,128)(2,1)S(1)}, u32[]{:S(2)}, u32[]{:S(2)}) async-start(bf16[16,32,256]{2,1,0:T(8,128)(2,1)} %broadcast_in_dim.57), calls=%async_computation.1 | async-start | bytes 524288 | tf_op jit(solution)/shard_map/all_to_all | solution.py:241
  36.8 0.7 copy-start.1
  36.8 13.3 %copy-start.2 = (s32[1,1,160]{2,1,0:T(1,128)S(1)}, s32[1,1,160]{2,1,0:T(1,128)}, u32[]{:S(2)}) copy-start(s32[1,1,160]{2,1,0:T(1,128)} %param.12) | copy-start | bytes 1924
  37.5 47.7 %all-to-all-start = ((bf16[128,32,256]{2,1,0:T(8,128)(2,1)}), bf16[128,32,256]{2,1,0:T(8,128)(2,1)S(1)}, u32[]{:S(2)}, u32[]{:S(2)}) async-start(bf16[128,32,256]{2,1,0:T(8,128)(2,1)} %bitcast.83), calls=%async_computation | async-start | bytes 4194304 | tf_op jit(solution)/shard_map/all_to_all | solution.py:245
  85.3 1.3 %copy-start = (bf16[128,32,256]{2,1,0:T(8,128)(2,1)}, bf16[128,32,256]{2,1,0:T(8,128)(2,1)S(1)}, u32[]{:S(2)}) copy-start(bf16[128,32,256]{2,1,0:T(8,128)(2,1)S(1)} %all-to-all-done) | copy-start | bytes 6291460
